TPU v7x, 32 devices: a whole 2x2x4 slice. The times are simulated.
32 devices in a mesh: req: 8 (over z, y), tp: 4 (over x, core).
Axes of the slice: x: 2, y: 2, z: 4, core: 2. Of those that a mesh axis runs over, the one named last changes fastest.
Arguments:
- hidden: bfloat16 [4096, 2048], P('req', 'tp'), may hold values from -6 to 6
- queries: bfloat16 [4096, 2048], P('req', 'tp'), may hold values from -4 to 4
- new_keys: bfloat16 [4096, 512], P('req'), may hold values from -4 to 4
- new_values: bfloat16 [4096, 512], P('req'), may hold values from -6 to 6
- cache_keys: bfloat16 [384, 64, 512], P('req'), may hold values from -6 to 6
- cache_values: bfloat16 [384, 64, 512], P('req'), may hold values from -6 to 6
- out_weight: bfloat16 [2048, 2048], P('tp'), may hold values from -0.125 to 0.125
- attn_gain: bfloat16 [2048], P('tp'), may hold values from 0.099609375 to 1.8984375
- ple_input: bfloat16 [4096, 256], P('req'), may hold values from -6 to 6
- ple_gate_weight: bfloat16 [2048, 256], P('tp'), may hold values from -0.125 to 0.125
- ple_proj_weight: bfloat16 [256, 2048], P(None, 'tp'), may hold values from -0.375 to 0.375
- ple_gain: bfloat16 [2048], P('tp'), may hold values from 0.099609375 to 1.8984375
- page_holder: int32 [384, 1], P('req'), may hold values from 0 to 7; in each aligned block of 48 rows (0 to 47, 48 to 95, ...) at most 6 rows name the same one
- page_slot: int32 [384, 1], P('req'), may hold values from 0 to 47
- page_counts: int32 [8, 8], P('req'), may hold values from 1 to 12, 48 in all within a row
- last_fill: int32 [8, 8], P('req'), may hold values from 1 to 64
- row_counts: int32 [8, 8], P('req'), may hold values from 1 to 256, 512 in all within a row
Outputs:
- layer_out: bfloat16 [4096, 2048], P('req', 'tp')
Inputs may be any that keep to these rules, and one draw needn't show every extreme that they name: `page_holder`: within the 48 page references of one device's requests (aligned blocks), no req index is named more than 6 times; in some block one is named exactly 6 times. `page_counts`: the 8 counts of one device sum to 48; some count equals 12. `row_counts`: the 8 counts of one device sum to 512; some count equals 256.
All inputs are finite; a program needn't handle non-finite values.
Results may differ from a plain program's by a relative error of at most 0.0061.
Values may be sent and summed in bfloat16 or wider, within the bound.
No kernel may reach another device: no remote copies, remote signals or barrier semaphores. Data moves between devices by JAX's collectives and lax.ppermute only.
A program may use at most 128 MiB of HBM per device.

v0:
```python
import math
import jax
import jax.numpy as jnp
from jax import lax
from jax.sharding import PartitionSpec as P

D = 2048
HD = 256


def slot_lookup(positions, counts):
    starts = jnp.cumsum(counts) - counts
    owning = jnp.sum((positions[:, None] >= starts[None, :]).astype(jnp.int32), axis=1) - 1
    return (owning, starts)


def table_pick(table, owning):
    onehot = owning[:, None] == jnp.arange(table.shape[0], dtype=jnp.int32)[None, :]
    return jnp.sum(jnp.where(onehot, table[None, :], 0), axis=1)


def attend_masks(counts_of_pages, fill_row, counts_of_rows, page_len, page_total, row_total):
    key_index = jnp.arange(page_total * page_len, dtype=jnp.int32)
    page_ref = key_index // page_len
    within = key_index % page_len
    page_owner, page_starts = slot_lookup(page_ref, counts_of_pages)
    context_len = (counts_of_pages - 1) * page_len + fill_row
    position = (page_ref - table_pick(page_starts, page_owner)) * page_len + within
    valid = position < table_pick(context_len, page_owner)
    row_index = jnp.arange(row_total, dtype=jnp.int32)
    row_owner = slot_lookup(row_index, counts_of_rows)[0]
    context_mask = (row_owner[:, None] == page_owner[None, :]) & valid[None, :]
    causal = (row_owner[:, None] == row_owner[None, :]) & (row_index[None, :] <= row_index[:, None])
    return jnp.concatenate([context_mask, causal], axis=1)


def shards(
    hidden,
    queries,
    new_keys,
    new_values,
    cache_keys,
    cache_values,
    out_weight,
    attn_gain,
    ple_input,
    ple_gate_weight,
    ple_proj_weight,
    ple_gain,
    page_holder,
    page_slot,
    page_counts,
    last_fill,
    row_counts,
):
    row_total = hidden.shape[0]
    page_total = cache_keys.shape[0]
    page_len = cache_keys.shape[1]
    req_count = lax.axis_size("req")
    tp_index = lax.axis_index("tp")
    local_heads = queries.shape[1] // HD
    kv_head = tp_index // 2
    capacity = max(2, page_total // req_count)
    holders = page_holder[:, 0]
    places = page_slot[:, 0]
    ref_index = jnp.arange(page_total, dtype=jnp.int32)
    earlier = (holders[:, None] == holders[None, :]) & (ref_index[:, None] > ref_index[None, :])
    ranking = jnp.sum(earlier.astype(jnp.int32), axis=1)
    matched = (holders[:, None, None] == jnp.arange(req_count, dtype=jnp.int32)[None, :, None]) & (
        ranking[:, None, None] == jnp.arange(capacity, dtype=jnp.int32)[None, None, :]
    )
    request_table = jnp.sum(jnp.where(matched, places[:, None, None] + 1, 0), axis=0) - 1
    asked = lax.all_to_all(request_table, "req", split_axis=0, concat_axis=0, tiled=True)
    wanted = jnp.maximum(asked, 0)
    head_keys = lax.dynamic_slice_in_dim(cache_keys, kv_head * HD, HD, 2)
    head_values = lax.dynamic_slice_in_dim(cache_values, kv_head * HD, HD, 2)
    stacked = jnp.concatenate([head_keys, head_values], axis=2)
    arrival_index = holders * capacity + ranking
    outgoing = stacked[wanted]
    arrived = lax.all_to_all(outgoing, "req", split_axis=0, concat_axis=0, tiled=True)
    context = arrived.reshape(req_count * capacity, page_len, 2 * HD)[arrival_index]
    context_keys = context[:, :, :HD].reshape(page_total * page_len, HD)
    context_values = context[:, :, HD:].reshape(page_total * page_len, HD)
    fresh_keys = lax.dynamic_slice_in_dim(new_keys, kv_head * HD, HD, 1)
    fresh_values = lax.dynamic_slice_in_dim(new_values, kv_head * HD, HD, 1)
    all_keys = jnp.concatenate([context_keys, fresh_keys], axis=0)
    all_values = jnp.concatenate([context_values, fresh_values], axis=0)
    masking = attend_masks(
        page_counts[0], last_fill[0], row_counts[0], page_len, page_total, row_total
    )
    query_rows = queries.reshape(row_total, local_heads, HD)
    scores = jnp.einsum("rhd,kd->hrk", query_rows, all_keys, preferred_element_type=jnp.float32) * (
        1.0 / math.sqrt(HD)
    )
    scores = jnp.where(masking[None], scores, -1e30)
    highest = jnp.max(scores, axis=-1, keepdims=True)
    expo = jnp.exp(scores - highest)
    weights = (expo / jnp.sum(expo, axis=-1, keepdims=True)).astype(jnp.bfloat16)
    attention = jnp.einsum("hrk,kd->rhd", weights, all_values, preferred_element_type=jnp.float32)
    attention = attention.astype(jnp.bfloat16).reshape(row_total, local_heads * HD)
    partial_sum = jnp.dot(attention, out_weight, preferred_element_type=jnp.float32)
    columns = hidden.shape[1]
    summed = lax.psum(partial_sum, "tp")
    squares = jnp.sum(summed * summed, axis=1)
    local_part = lax.dynamic_slice_in_dim(summed, tp_index * columns, columns, 1)
    normed = (
        local_part
        * lax.rsqrt(squares / D + 1e-06)[:, None]
        * attn_gain.astype(jnp.float32)[None, :]
    )
    mixed_state = (hidden.astype(jnp.float32) + normed).astype(jnp.bfloat16)
    gate = lax.psum(jnp.dot(mixed_state, ple_gate_weight, preferred_element_type=jnp.float32), "tp")
    activated = (jax.nn.gelu(gate, approximate=True) * ple_input.astype(jnp.float32)).astype(
        jnp.bfloat16
    )
    lifted = jnp.dot(activated, ple_proj_weight, preferred_element_type=jnp.float32)
    lift_squares = lax.psum(jnp.sum(lifted * lifted, axis=1), "tp")
    lift_normed = (
        lifted
        * lax.rsqrt(lift_squares / D + 1e-06)[:, None]
        * ple_gain.astype(jnp.float32)[None, :]
    )
    return (mixed_state.astype(jnp.float32) + lift_normed).astype(jnp.bfloat16)


def solution(mesh):
    return jax.shard_map(
        shards,
        mesh=mesh,
        in_specs=(
            P("req", "tp"),
            P("req", "tp"),
            P("req", None),
            P("req", None),
            P("req", None, None),
            P("req", None, None),
            P("tp", None),
            P("tp"),
            P("req", None),
            P("tp", None),
            P(None, "tp"),
            P("tp"),
            P("req", None),
            P("req", None),
            P("req", None),
            P("req", None),
            P("req", None),
        ),
        out_specs=P("req", "tp"),
        check_vma=False,
    )
```

profile of v0, /device:TPU:0, one launch (start us, length us, event | category | flops | bytes accessed | tf_op | source)
XLA Modules:
  0.0 293.5 jit_solution(17418125813564555138)
XLA Ops:
  6.5 1.0 convert_reduce_fusion.1
  7.5 0.7 iota_compare_fusion.5
  8.2 0.7 add_bitcast_fusion.2
  8.9 0.2 select_reduce_fusion.2
  9.1 0.7 copy.35
  9.7 7.3 %all-to-all-start = ((s32[8,1,6]{2,1,0:T(1,128)}), s32[8,1,6]{2,1,0:T(1,128)S(1)}, u32[]{:S(2)}, u32[]{:S(2)}) async-start(s32[8,1,6]{2,1,0:T(1,128)} %copy.35), calls=%async_computation | async-start | bytes 8192 | tf_op jit(solution)/shard_map/all_to_all | solution.py:73
  17.0 2.2 constant_dynamic-slice_fusion.2
  19.3 2.0 pad_maximum_fusion
  21.2 2.2 all-to-all-done
  23.4 0.1 reshape.180
  23.5 4.4 %gather_fusion = bf16[48,64,512]{2,1,0:T(8,128)(2,1)} fusion(bf16[48,64,512]{2,1,0:T(8,128)(2,1)} %pad_maximum_fusion, s32[1024]{0:T(1024)S(1)} %pad_clamp_fusion.1), kind=kCustom, calls=%fused_computation | custom fusion | bytes 6291648 | tf_op jit(solution)/shard_map/gather | solution.py:79
  28.0 0.0 copy-start.7
  28.0 4.6 %all-to-all-start.1 = ((bf16[8,6,64,512]{3,2,1,0:T(8,128)(2,1)}), bf16[8,6,64,512]{3,2,1,0:T(8,128)(2,1)}, u32[]{:S(2)}, u32[]{:S(2)}) async-start(bf16[8,6,64,512]{3,2,1,0:T(8,128)(2,1)} %bitcast.52), calls=%async_computation.1 | async-start | bytes 6291456 | tf_op jit(solution)/shard_map/all_to_all | solution.py:80
  32.6 0.0 all-reduce.3.cloned.1.call-start
  32.6 0.0 copy-done.8
  32.6 0.2 reduce-window_1_clone.1
  32.8 0.0 copy-done.10
  32.8 0.2 reduce-window_clone.1
  33.0 1.0 constant_dynamic-slice_fusion
  34.0 0.1 copy.44
  34.2 0.1 convert_reduce_fusion.2
  34.3 0.1 convert_reduce_fusion
  34.4 0.1 select_reduce_fusion.1
  34.6 0.2 fusion.12
  34.8 2.4 compare_and_fusion
  37.1 1.7 pad_add_fusion
  38.8 63.4 %all-to-all-done.1 = bf16[8,6,64,512]{3,2,1,0:T(8,128)(2,1)} async-done(((bf16[8,6,64,512]{3,2,1,0:T(8,128)(2,1)}), bf16[8,6,64,512]{3,2,1,0:T(8,128)(2,1)}, u32[]{:S(2)}, u32[]{:S(2)}) %all-to-all-start.1) | async-done | bytes 3145760 | tf_op jit(solution)/shard_map/all_to_all | solution.py:80
  102.2 4.4 %gather_fusion.1 = bf16[48,64,512]{2,1,0:T(8,128)(2,1)} fusion(bf16[48,64,512]{2,1,0:T(8,128)(2,1)} %bitcast.4, s32[1024]{0:T(1024)S(1)} %pad_clamp_fusion), kind=kCustom, calls=%fused_computation.1 | custom fusion | bytes 6291648 | tf_op jit(solution)/shard_map/gather | solution.py:81
  106.7 4.0 %fusion.49 = (bf16[48,64,256]{2,1,0:T(8,128)(2,1)}, bf16[48,64,256]{2,1,0:T(8,128)(2,1)}) fusion(bf16[48,64,512]{2,1,0:T(8,128)(2,1)} %gather_fusion.1), kind=kLoop, calls=%fused_computation.97 | loop fusion | bytes 6291456 | tf_op jit(solution)/shard_map/slice | solution.py:83
  110.6 2.7 copy.37
  113.3 8.7 %fusion.8 = f32[3584,512,2]{1,0,2:T(8,128)} fusion(bf16[512,256]{1,0:T(8,128)(2,1)S(1)} %get-tuple-element.15, bf16[3072,256]{1,0:T(8,128)(2,1)} %bitcast.53, bf16[64,2,8,256]{3,2,1,0:T(8,128)(2,1)S(1)} %bitcast.55), kind=kOutput, calls=%fused_computation.19 | convolution fusion | flops 1882718208 | bytes 17039360 | tf_op jit(solution)/shard_map/rhd,kd->hrk/dot_general | solution.py:92
  122.0 17.1 %fusion.50 = (f32[2,512]{1,0:T(2,128)S(1)}, f32[2,512,3584]{1,2,0:T(8,128)}) fusion(f32[3584,512,2]{1,0,2:T(8,128)} %fusion.8, pred[512,3584]{0,1:T(8,128)(4,1)} %pad_add_fusion), kind=kOutput, calls=%fused_computation.98 | output fusion | flops 22023680 | bytes 31199232 | tf_op jit(solution)/shard_map/sub | solution.py:97
  139.1 7.7 %fusion.11 = bf16[256,2,512]{2,0,1:T(8,128)(2,1)S(1)} fusion(f32[2,512,3584]{1,2,0:T(8,128)} %get-tuple-element.12, f32[2,512]{1,0:T(2,128)S(1)} %get-tuple-element.11, bf16[512,256]{0,1:T(8,128)(2,1)S(1)} %copy.44, bf16[3072,256]{0,1:T(8,128)(2,1)} %copy.37), kind=kOutput, calls=%fused_computation.22 | convolution fusion | flops 1890320384 | bytes 17043456 | tf_op jit(solution)/shard_map/hrk,kd->rhd/dot_general | solution.py:99
  146.9 3.2 %fusion.51 = f32[512,2048]{1,0:T(8,128)} fusion(bf16[512,512]{0,1:T(8,128)(2,1)S(1)} %bitcast.56, bf16[512,2048]{1,0:T(8,128)(2,1)S(1)} %copy-done), kind=kOutput, calls=%fused_computation.99 | convolution fusion | flops 1073741824 | bytes 6815744 | tf_op jit(solution)/shard_map/dot_general | solution.py:101
  150.1 0.0 all-reduce.3.cloned.1.call-update
  150.1 0.0 copy-start.2
  150.1 0.0 all-reduce.5.cloned.1.call-start
  150.2 0.6 copy-done.5
  150.8 84.0 %all-reduce.3.cloned.1.call-done = f32[512,2048]{1,0:T(8,128)} async-done(((f32[512,2048]{1,0:T(8,128)}), f32[512,2048]{1,0:T(8,128)}) %all-reduce.3.cloned.1.call-update) | async-done | bytes 4194320 | tf_op jit(solution)/shard_map/psum | solution.py:103
  234.8 2.5 multiply_reduce_fusion
  237.4 1.5 add_convert_fusion.1
  238.8 1.1 fusion.52
  239.9 0.0 all-reduce.5.cloned.1.call-update
  240.0 33.5 %all-reduce.5.cloned.1.call-done = f32[512,256]{1,0:T(8,128)} async-done(((f32[512,256]{1,0:T(8,128)}), f32[512,256]{1,0:T(8,128)}) %all-reduce.5.cloned.1.call-update) | async-done | bytes 524304 | tf_op jit(solution)/shard_map/psum | solution.py:112
  273.4 2.7 multiply_reduce_fusion.1
  276.1 2.6 copy.40
  278.7 5.7 %psum.23 = f32[512]{0:T(512)S(1)} all-reduce(f32[512]{0:T(512)S(1)} %get-tuple-element.13), channel_id=1, replica_groups=mesh['req'=8,'tp'=4] {'tp'}, use_global_device_ids=true, to_apply=%region_14.15 | all-reduce | flops 512 | bytes 4096 | tf_op jit(solution)/shard_map/psum | solution.py:117
  284.4 2.2 add_convert_fusion
  (33 shorter events, 0.1 us)
Async XLA Ops:
  6.5 140.3 %copy-start = (bf16[512,2048]{1,0:T(8,128)(2,1)S(1)}, bf16[512,2048]{1,0:T(8,128)(2,1)}, u32[]{:S(2)}) copy-start(bf16[512,2048]{1,0:T(8,128)(2,1)} %param.23) | copy-start | bytes 6291460
  9.7 13.7 %all-to-all-start = ((s32[8,1,6]{2,1,0:T(1,128)}), s32[8,1,6]{2,1,0:T(1,128)S(1)}, u32[]{:S(2)}, u32[]{:S(2)}) async-start(s32[8,1,6]{2,1,0:T(1,128)} %copy.35), calls=%async_computation | async-start | bytes 8192 | tf_op jit(solution)/shard_map/all_to_all | solution.py:73
  28.0 4.7 %copy-start.8 = (s32[1,8]{1,0:T(1,128)S(1)}, s32[1,8]{1,0:T(1,128)}, u32[]{:S(2)}) copy-start(s32[1,8]{1,0:T(1,128)} %param.31) | copy-start | bytes 100
  28.0 4.9 %copy-start.10 = (s32[1,8]{1,0:T(1,128)S(1)}, s32[1,8]{1,0:T(1,128)}, u32[]{:S(2)}) copy-start(s32[1,8]{1,0:T(1,128)} %param.33) | copy-start | bytes 100
  28.0 5.0 %copy-start.4 = (bf16[512,512]{1,0:T(8,128)(2,1)S(1)}, bf16[512,512]{1,0:T(8,128)(2,1)}, u32[]{:S(2)}) copy-start(bf16[512,512]{1,0:T(8,128)(2,1)} %param.19) | copy-start | bytes 1572868
  28.0 6.2 %copy-start.9 = (s32[48,1]{0,1:T(1,128)S(1)}, s32[48,1]{0,1:T(1,128)}, u32[]{:S(2)}) copy-start(s32[48,1]{0,1:T(1,128)} %param.29) | copy-start | bytes 580
  28.0 6.3 %copy-start.7 = (s32[1,8]{1,0:T(1,128)S(1)}, s32[1,8]{1,0:T(1,128)}, u32[]{:S(2)}) copy-start(s32[1,8]{1,0:T(1,128)} %param.32) | copy-start | bytes 100
  28.0 74.2 %all-to-all-start.1 = ((bf16[8,6,64,512]{3,2,1,0:T(8,128)(2,1)}), bf16[8,6,64,512]{3,2,1,0:T(8,128)(2,1)}, u32[]{:S(2)}, u32[]{:S(2)}) async-start(bf16[8,6,64,512]{3,2,1,0:T(8,128)(2,1)} %bitcast.52), calls=%async_computation.1 | async-start | bytes 6291456 | tf_op jit(solution)/shard_map/all_to_all | solution.py:80
  32.6 202.2 %all-reduce.3.cloned.1.call-start = ((), (), s32[]{:S(2)}) async-start(), calls=%async_computation.2 | async-start | bytes 8388608 | tf_op jit(solution)/shard_map/psum | solution.py:103
  110.6 2.7 copy-start.1
  150.1 0.7 copy-start.5
  150.1 87.2 %copy-start.2 = (bf16[512,512]{1,0:T(8,128)(2,1)S(1)}, bf16[512,512]{1,0:T(8,128)(2,1)}, u32[]{:S(2)}) copy-start(bf16[512,512]{1,0:T(8,128)(2,1)} %param.17) | copy-start | bytes 1572868
  150.1 123.3 %all-reduce.5.cloned.1.call-start = ((), (), s32[]{:S(2)}) async-start(), calls=%async_computation.3 | async-start | bytes 1048576 | tf_op jit(solution)/shard_map/psum | solution.py:112
  150.8 88.0 %copy-start.3 = (bf16[512,256]{1,0:T(8,128)(2,1)S(1)}, bf16[512,256]{1,0:T(8,128)(2,1)}, u32[]{:S(2)}) copy-start(bf16[512,256]{1,0:T(8,128)(2,1)} %param.26) | copy-start | bytes 786436
  150.8 89.2 %copy-start.6 = (bf16[512]{0:T(512)(128)(2,1)S(1)}, bf16[512]{0:T(512)(128)(2,1)}, u32[]{:S(2)}) copy-start(bf16[512]{0:T(512)(128)(2,1)} %param.28) | copy-start | bytes 3076
Sparse Core Ops, SparseCore 0:
  150.3 84.5 all-reduce.2
  240.1 33.3 all-reduce.4
where the time goes:
time: 294 us
  waiting for transfers between devices  183 us (62%)
  other arithmetic  32.8 us (11%)
  matrix products  23.5 us (8%)
  local copies, waits for them, and re-layouts  22.9 us (8%)
  between operations  13.6 us (5%)
  starting transfers between devices  11.9 us (4%)
  blocking collectives  5.73 us (2%)
    psum x1, waiting for transfers between devices, shards(): summed = lax.psum(partial_sum, 'tp')  84 us
    all_to_all x1, waiting for transfers between devices, shards(): lax.all_to_all(outgoing, 'req', split_axis=0, concat_axis=0, tiled=True)  63.4 us
    psum x1, waiting for transfers between devices, shards(): lax.psum(jnp.dot(mixed_state, ple_gate_weight, preferred_element_type=jnp...  33.5 us
    sub x1, other arithmetic, shards(): expo = jnp.exp(scores - highest)  17.1 us
    dot_general x1, matrix products, shards(): jnp.einsum('rhd,kd->hrk', query_rows, all_keys, preferred_element_type=jn...  8.73 us
    dot_general x1, matrix products, shards(): jnp.einsum('hrk,kd->rhd', weights, all_values, preferred_element_type=jnp...  7.72 us
    all_to_all x1, starting transfers between devices, shards(): lax.all_to_all(request_table, 'req', split_axis=0, concat_axis=0, tiled=T...  7.28 us
  transfers between devices with their start and end apart: 4, of which 4 were waited for; matrix products, arithmetic and copies ran while one was open for 4% of the time, Pallas kernels for 0%

commit v1 on v0

--- a/solution.py
+++ b/solution.py
@@ -70,7 +70,21 @@
         ranking[:, None, None] == jnp.arange(capacity, dtype=jnp.int32)[None, None, :]
     )
     request_table = jnp.sum(jnp.where(matched, places[:, None, None] + 1, 0), axis=0) - 1
-    asked = lax.all_to_all(request_table, "req", split_axis=0, concat_axis=0, tiled=True)
+    v_now = lax.axis_index("req")
+    near = lax.axis_size("req")
+    block_last, placed = (near, v_now)
+    w2 = request_table.shape[0] // block_last
+    raw_out = jnp.roll(request_table, -placed * w2, 0)
+    plain = lax.slice_in_dim(raw_out, 0, w2, axis=0)
+    by_rank = [plain]
+    for ix in range(1, block_last):
+        z_new = lax.slice_in_dim(raw_out, ix * w2, (ix + 1) * w2, axis=0)
+        long_array = lax.ppermute(
+            z_new, "req", [(kk, (kk + ix) % block_last) for kk in range(block_last)]
+        )
+        by_rank.append(long_array)
+    block_now = jnp.concatenate(by_rank[::-1], 0)
+    asked = jnp.roll(block_now, (placed + 1) * by_rank[0].shape[0], axis=0)
     wanted = jnp.maximum(asked, 0)
     head_keys = lax.dynamic_slice_in_dim(cache_keys, kv_head * HD, HD, 2)
     head_values = lax.dynamic_slice_in_dim(cache_values, kv_head * HD, HD, 2)

time: 294 us -> 301 us (1.024)
  starting transfers between devices: 11.9 us -> 17.1 us
    ppermute x0 -> x7, starting transfers between devices: none -> 12.4 us  [shards(): lax.ppermute(z_new, 'req', [(kk, (kk + ix) % block_last) for kk in range(...]
    all_to_all x1 -> x0, starting transfers between devices: 7.28 us -> none  [shards(): lax.all_to_all(request_table, 'req', split_axis=0, concat_axis=0, tiled=T...]
    ppermute x0 -> x7, waiting for transfers between devices: none -> 5.17 us  [shards(): lax.ppermute(z_new, 'req', [(kk, (kk + ix) % block_last) for kk in range(...]
  transfers between devices with their start and end apart: 4 -> 10, of which waited for: 4 -> 5; matrix products, arithmetic and copies ran while one was open for 4% -> 3% of each run, Pallas kernels for 0% -> 0%
where the time goes in v1:
time: 301 us; the launch traced here: 300 us
  waiting for transfers between devices  185 us (61%)
  other arithmetic  33 us (11%)
  matrix products  23.5 us (8%)
  local copies, waits for them, and re-layouts  22.5 us (7%)
  starting transfers between devices  17.1 us (6%)
  between operations  13.6 us (5%)
  blocking collectives  5.73 us (2%)
    psum x1, waiting for transfers between devices, shards(): summed = lax.psum(partial_sum, 'tp')  84 us
    all_to_all x1, waiting for transfers between devices, shards(): lax.all_to_all(outgoing, 'req', split_axis=0, concat_axis=0, tiled=True)  61.9 us
    psum x1, waiting for transfers between devices, shards(): lax.psum(jnp.dot(mixed_state, ple_gate_weight, preferred_element_type=jnp...  33.5 us
    sub x1, other arithmetic, shards(): expo = jnp.exp(scores - highest)  17.1 us
    ppermute x7, starting transfers between devices, shards(): lax.ppermute(z_new, 'req', [(kk, (kk + ix) % block_last) for kk in range(...  12.4 us
    dot_general x1, matrix products, shards(): jnp.einsum('rhd,kd->hrk', query_rows, all_keys, preferred_element_type=jn...  8.73 us
    dot_general x1, matrix products, shards(): jnp.einsum('hrk,kd->rhd', weights, all_values, preferred_element_type=jnp...  7.72 us
  transfers between devices with their start and end apart: 10, of which 5 were waited for; matrix products, arithmetic and copies ran while one was open for 3% of the time, Pallas kernels for 0%

profile of v1, /device:TPU:0, one launch (start us, length us, event | category | flops | bytes accessed | tf_op | source)
XLA Modules:
  0.0 300.0 jit_solution(2314647680060880362)
XLA Ops:
  6.5 1.0 convert_reduce_fusion.1
  7.5 0.7 iota_compare_fusion.5
  8.2 0.7 add_bitcast_fusion.1
  8.9 0.2 select_reduce_fusion.2
  9.2 0.1 fusion.50
  9.3 6.0 %collective-permute-start = (s32[1,6]{0,1:T(8,128)S(1)}, s32[1,6]{0,1:T(8,128)S(1)}, u32[]{:S(2)}, u32[]{:S(2)}) collective-permute-start(s32[1,6]{0,1:T(8,128)S(1)} %get-tuple-element.17), channel_id=1, source_target_pairs={{0,28},{4,0},{8,4},{12,8},{16,12},{20,16},{24,20},{28,24},{1,29},{... | collective-permute-start | bytes 80 | tf_op jit(solution)/shard_map/ppermute | solution.py:82
  15.3 0.4 collective-permute-start.1
  15.8 3.0 collective-permute-start.3
  18.7 2.2 constant_dynamic-slice_fusion.3
  21.0 2.0 pad_maximum_fusion
  23.0 1.9 collective-permute-start.5
  24.8 1.1 collective-permute-start.6
  26.0 3.4 %collective-permute-done.5 = s32[1,6]{0,1:T(8,128)S(1)} collective-permute-done((s32[1,6]{0,1:T(8,128)S(1)}, s32[1,6]{0,1:T(8,128)S(1)}, u32[]{:S(2)}, u32[]{:S(2)}) %collective-permute-start.5) | collective-permute-done | bytes 56 | tf_op jit(solution)/shard_map/ppermute | solution.py:82
  29.3 1.8 collective-permute-done.6
  31.1 0.1 concatenate.19
  31.2 0.1 pad_add_fusion.2
  31.4 0.1 copy.28
  31.4 0.1 reshape.157
  31.5 4.4 %gather_fusion = bf16[48,64,512]{2,1,0:T(8,128)(2,1)} fusion(bf16[48,64,512]{2,1,0:T(8,128)(2,1)} %pad_maximum_fusion, s32[1024]{0:T(1024)S(1)} %pad_clamp_fusion.1), kind=kCustom, calls=%fused_computation | custom fusion | bytes 6291648 | tf_op jit(solution)/shard_map/gather | solution.py:93
  36.0 4.6 %all-to-all-start = ((bf16[8,6,64,512]{3,2,1,0:T(8,128)(2,1)}), bf16[8,6,64,512]{3,2,1,0:T(8,128)(2,1)}, u32[]{:S(2)}, u32[]{:S(2)}) async-start(bf16[8,6,64,512]{3,2,1,0:T(8,128)(2,1)} %bitcast.50), calls=%async_computation | async-start | bytes 6291456 | tf_op jit(solution)/shard_map/all_to_all | solution.py:94
  40.6 0.2 reduce-window_1_clone.1
  40.8 0.2 reduce-window_clone.1
  41.0 1.0 constant_dynamic-slice_fusion.1
  42.0 0.1 copy.35
  42.2 0.1 convert_reduce_fusion.2
  42.3 0.1 convert_reduce_fusion
  42.4 0.1 select_reduce_fusion.1
  42.6 0.2 fusion.12
  42.8 2.4 compare_and_fusion
  45.1 1.7 pad_add_fusion
  46.8 61.9 %all-to-all-done = bf16[8,6,64,512]{3,2,1,0:T(8,128)(2,1)} async-done(((bf16[8,6,64,512]{3,2,1,0:T(8,128)(2,1)}), bf16[8,6,64,512]{3,2,1,0:T(8,128)(2,1)}, u32[]{:S(2)}, u32[]{:S(2)}) %all-to-all-start) | async-done | bytes 3145760 | tf_op jit(solution)/shard_map/all_to_all | solution.py:94
  108.7 4.4 %gather_fusion.1 = bf16[48,64,512]{2,1,0:T(8,128)(2,1)} fusion(bf16[48,64,512]{2,1,0:T(8,128)(2,1)} %bitcast.3, s32[1024]{0:T(1024)S(1)} %pad_clamp_fusion), kind=kCustom, calls=%fused_computation.1 | custom fusion | bytes 6291648 | tf_op jit(solution)/shard_map/gather | solution.py:95
  113.2 4.0 %fusion.49 = (bf16[48,64,256]{2,1,0:T(8,128)(2,1)}, bf16[48,64,256]{2,1,0:T(8,128)(2,1)}) fusion(bf16[48,64,512]{2,1,0:T(8,128)(2,1)} %gather_fusion.1), kind=kLoop, calls=%fused_computation.100 | loop fusion | bytes 6291456 | tf_op jit(solution)/shard_map/slice | solution.py:97
  117.2 2.7 copy.30
  119.8 8.7 %fusion.8 = f32[3584,512,2]{1,0,2:T(8,128)} fusion(bf16[512,256]{1,0:T(8,128)(2,1)S(1)} %get-tuple-element.24, bf16[3072,256]{1,0:T(8,128)(2,1)} %bitcast.51, bf16[64,2,8,256]{3,2,1,0:T(8,128)(2,1)S(1)} %bitcast.53), kind=kOutput, calls=%fused_computation.19 | convolution fusion | flops 1882718208 | bytes 17039360 | tf_op jit(solution)/shard_map/rhd,kd->hrk/dot_general | solution.py:106
  128.6 17.1 %fusion.51 = (f32[2,512]{1,0:T(2,128)S(1)}, f32[2,512,3584]{1,2,0:T(8,128)}) fusion(f32[3584,512,2]{1,0,2:T(8,128)} %fusion.8, pred[512,3584]{0,1:T(8,128)(4,1)} %pad_add_fusion), kind=kOutput, calls=%fused_computation.102 | output fusion | flops 22023680 | bytes 31199232 | tf_op jit(solution)/shard_map/sub | solution.py:111
  145.6 7.7 %fusion.11 = bf16[256,2,512]{2,0,1:T(8,128)(2,1)S(1)} fusion(f32[2,512,3584]{1,2,0:T(8,128)} %get-tuple-element.21, f32[2,512]{1,0:T(2,128)S(1)} %get-tuple-element.20, bf16[512,256]{0,1:T(8,128)(2,1)S(1)} %copy.35, bf16[3072,256]{0,1:T(8,128)(2,1)} %copy.30), kind=kOutput, calls=%fused_computation.22 | convolution fusion | flops 1890320384 | bytes 17043456 | tf_op jit(solution)/shard_map/hrk,kd->rhd/dot_general | solution.py:113
  153.4 3.2 %fusion.52 = f32[512,2048]{1,0:T(8,128)} fusion(bf16[512,512]{0,1:T(8,128)(2,1)S(1)} %bitcast.54, bf16[512,2048]{1,0:T(8,128)(2,1)S(1)} %copy-done), kind=kOutput, calls=%fused_computation.103 | convolution fusion | flops 1073741824 | bytes 6815744 | tf_op jit(solution)/shard_map/dot_general | solution.py:115
  156.7 0.6 copy-done.5
  157.3 84.0 %all-reduce.3.cloned.1.call-done = f32[512,2048]{1,0:T(8,128)} async-done(((f32[512,2048]{1,0:T(8,128)}), f32[512,2048]{1,0:T(8,128)}) %all-reduce.3.cloned.1.call-update) | async-done | bytes 4194320 | tf_op jit(solution)/shard_map/psum | solution.py:117
  241.3 2.5 multiply_reduce_fusion
  243.9 1.5 add_convert_fusion.1
  245.3 1.1 fusion.53
  246.5 33.5 %all-reduce.5.cloned.1.call-done = f32[512,256]{1,0:T(8,128)} async-done(((f32[512,256]{1,0:T(8,128)}), f32[512,256]{1,0:T(8,128)}) %all-reduce.5.cloned.1.call-update) | async-done | bytes 524304 | tf_op jit(solution)/shard_map/psum | solution.py:126
  279.9 2.7 multiply_reduce_fusion.1
  282.6 2.6 copy.33
  285.2 5.7 %psum.23 = f32[512]{0:T(512)S(1)} all-reduce(f32[512]{0:T(512)S(1)} %get-tuple-element.22), channel_id=1, replica_groups=mesh['req'=8,'tp'=4] {'tp'}, use_global_device_ids=true, to_apply=%region_14.16 | all-reduce | flops 512 | bytes 4096 | tf_op jit(solution)/shard_map/psum | solution.py:131
  290.9 2.2 add_convert_fusion
  (50 shorter events, 0.5 us)
Async XLA Ops:
  6.5 146.8 %copy-start = (bf16[512,2048]{1,0:T(8,128)(2,1)S(1)}, bf16[512,2048]{1,0:T(8,128)(2,1)}, u32[]{:S(2)}) copy-start(bf16[512,2048]{1,0:T(8,128)(2,1)} %param.25) | copy-start | bytes 6291460
  9.3 13.7 %collective-permute-start = (s32[1,6]{0,1:T(8,128)S(1)}, s32[1,6]{0,1:T(8,128)S(1)}, u32[]{:S(2)}, u32[]{:S(2)}) collective-permute-start(s32[1,6]{0,1:T(8,128)S(1)} %get-tuple-element.17), channel_id=1, source_target_pairs={{0,28},{4,0},{8,4},{12,8},{16,12},{20,16},{24,20},{28,24},{1,29},{... | collective-permute-start | bytes 80 | tf_op jit(solution)/shard_map/ppermute | solution.py:82
  15.3 9.5 %collective-permute-start.1 = (s32[1,6]{0,1:T(8,128)S(1)}, s32[1,6]{0,1:T(8,128)S(1)}, u32[]{:S(2)}, u32[]{:S(2)}) collective-permute-start(s32[1,6]{0,1:T(8,128)S(1)} %get-tuple-element.16), channel_id=1, source_target_pairs={{0,24},{4,28},{8,0},{12,4},{16,8},{20,12},{24,16},{28,20},{1,25},{... | collective-permute-start | bytes 80 | tf_op jit(solution)/shard_map/ppermute | solution.py:82
  15.8 10.2 %collective-permute-start.2 = (s32[1,6]{0,1:T(8,128)S(1)}, s32[1,6]{0,1:T(8,128)S(1)}, u32[]{:S(2)}, u32[]{:S(2)}) collective-permute-start(s32[1,6]{0,1:T(8,128)S(1)} %get-tuple-element.15), channel_id=1, source_target_pairs={{0,20},{4,24},{8,28},{12,0},{16,4},{20,8},{24,12},{28,16},{1,21},{... | collective-permute-start | bytes 80 | tf_op jit(solution)/shard_map/ppermute | solution.py:82
  15.8 10.2 %collective-permute-start.3 = (s32[1,6]{0,1:T(8,128)S(1)}, s32[1,6]{0,1:T(8,128)S(1)}, u32[]{:S(2)}, u32[]{:S(2)}) collective-permute-start(s32[1,6]{0,1:T(8,128)S(1)} %get-tuple-element.14), channel_id=1, source_target_pairs={{0,16},{4,20},{8,24},{12,28},{16,0},{20,4},{24,8},{28,12},{1,17},{... | collective-permute-start | bytes 80 | tf_op jit(solution)/shard_map/ppermute | solution.py:82
  18.7 7.2 %collective-permute-start.4 = (s32[1,6]{0,1:T(8,128)S(1)}, s32[1,6]{0,1:T(8,128)S(1)}, u32[]{:S(2)}, u32[]{:S(2)}) collective-permute-start(s32[1,6]{0,1:T(8,128)S(1)} %get-tuple-element.13), channel_id=1, source_target_pairs={{0,12},{4,16},{8,20},{12,24},{16,28},{20,0},{24,4},{28,8},{1,13},{... | collective-permute-start | bytes 80 | tf_op jit(solution)/shard_map/ppermute | solution.py:82
  23.0 6.4 %collective-permute-start.5 = (s32[1,6]{0,1:T(8,128)S(1)}, s32[1,6]{0,1:T(8,128)S(1)}, u32[]{:S(2)}, u32[]{:S(2)}) collective-permute-start(s32[1,6]{0,1:T(8,128)S(1)} %get-tuple-element.12), channel_id=1, source_target_pairs={{0,8},{4,12},{8,16},{12,20},{16,24},{20,28},{24,0},{28,4},{1,9},{5... | collective-permute-start | bytes 80 | tf_op jit(solution)/shard_map/ppermute | solution.py:82
  24.8 6.3 %collective-permute-start.6 = (s32[1,6]{0,1:T(8,128)S(1)}, s32[1,6]{0,1:T(8,128)S(1)}, u32[]{:S(2)}, u32[]{:S(2)}) collective-permute-start(s32[1,6]{0,1:T(8,128)S(1)} %get-tuple-element.11), channel_id=1, source_target_pairs={{0,4},{4,8},{8,12},{12,16},{16,20},{20,24},{24,28},{28,0},{1,5},{5... | collective-permute-start | bytes 80 | tf_op jit(solution)/shard_map/ppermute | solution.py:82
  36.0 4.7 %copy-start.8 = (s32[1,8]{1,0:T(1,128)S(1)}, s32[1,8]{1,0:T(1,128)}, u32[]{:S(2)}) copy-start(s32[1,8]{1,0:T(1,128)} %param.33) | copy-start | bytes 100
  36.0 4.9 %copy-start.10 = (s32[1,8]{1,0:T(1,128)S(1)}, s32[1,8]{1,0:T(1,128)}, u32[]{:S(2)}) copy-start(s32[1,8]{1,0:T(1,128)} %param.35) | copy-start | bytes 100
  36.0 5.0 %copy-start.4 = (bf16[512,512]{1,0:T(8,128)(2,1)S(1)}, bf16[512,512]{1,0:T(8,128)(2,1)}, u32[]{:S(2)}) copy-start(bf16[512,512]{1,0:T(8,128)(2,1)} %param.21) | copy-start | bytes 1572868
  36.0 6.2 %copy-start.9 = (s32[48,1]{0,1:T(1,128)S(1)}, s32[48,1]{0,1:T(1,128)}, u32[]{:S(2)}) copy-start(s32[48,1]{0,1:T(1,128)} %param.31) | copy-start | bytes 580
  36.0 6.3 %copy-start.7 = (s32[1,8]{1,0:T(1,128)S(1)}, s32[1,8]{1,0:T(1,128)}, u32[]{:S(2)}) copy-start(s32[1,8]{1,0:T(1,128)} %param.34) | copy-start | bytes 100
  36.0 72.7 %all-to-all-start = ((bf16[8,6,64,512]{3,2,1,0:T(8,128)(2,1)}), bf16[8,6,64,512]{3,2,1,0:T(8,128)(2,1)}, u32[]{:S(2)}, u32[]{:S(2)}) async-start(bf16[8,6,64,512]{3,2,1,0:T(8,128)(2,1)} %bitcast.50), calls=%async_computation | async-start | bytes 6291456 | tf_op jit(solution)/shard_map/all_to_all | solution.py:94
  40.6 200.7 %all-reduce.3.cloned.1.call-start = ((), (), s32[]{:S(2)}) async-start(), calls=%async_computation.1 | async-start | bytes 8388608 | tf_op jit(solution)/shard_map/psum | solution.py:117
  117.2 2.7 copy-start.1
  156.6 0.7 copy-start.5
  156.7 87.2 %copy-start.2 = (bf16[512,512]{1,0:T(8,128)(2,1)S(1)}, bf16[512,512]{1,0:T(8,128)(2,1)}, u32[]{:S(2)}) copy-start(bf16[512,512]{1,0:T(8,128)(2,1)} %param.19) | copy-start | bytes 1572868
  156.7 123.3 %all-reduce.5.cloned.1.call-start = ((), (), s32[]{:S(2)}) async-start(), calls=%async_computation.2 | async-start | bytes 1048576 | tf_op jit(solution)/shard_map/psum | solution.py:126
  157.3 88.0 %copy-start.3 = (bf16[512,256]{1,0:T(8,128)(2,1)S(1)}, bf16[512,256]{1,0:T(8,128)(2,1)}, u32[]{:S(2)}) copy-start(bf16[512,256]{1,0:T(8,128)(2,1)} %param.28) | copy-start | bytes 786436
  157.3 89.1 %copy-start.6 = (bf16[512]{0:T(512)(128)(2,1)S(1)}, bf16[512]{0:T(512)(128)(2,1)}, u32[]{:S(2)}) copy-start(bf16[512]{0:T(512)(128)(2,1)} %param.30) | copy-start | bytes 3076
Sparse Core Ops, SparseCore 0:
  156.8 84.4 all-reduce.2
  246.6 33.3 all-reduce.4
